TPU v7x, 128 devices: a whole 4x4x4 slice. The times are simulated.
128 devices in a mesh: blk: 8 (over z, x_lo), rep: 16 (over x_hi, y, core).
Axes of the slice: x: 4 (x_hi: 2, x_lo: 2; x = x_hi * 2 + x_lo), y: 4, z: 4, core: 2. Of those that a mesh axis runs over, the one named last changes fastest.
Arguments:
- raw_features: bfloat16 [131072, 512], P(('blk', 'rep')), may hold values from -6 to 6
- move_plan: int32 [8, 16, 16], P('blk'), may hold values from 8 to 64, as said below
- weight: bfloat16 [512, 512], replicated, may hold values from -0.25 to 0.25
- bias_vector: float32 [512], replicated, may hold values from -3 to 3
- tile_rows: int32 [8, 16, 16, 6], P('blk', 'rep'), may hold values from 0 to 31, as said below
- tile_values: bfloat16 [8, 16, 16, 6, 256, 256], P('blk', 'rep'), may hold values from -0.0546875 to 0.0546875
- grad_out: bfloat16 [65536, 512], P(('blk', 'rep')), may hold values from -6 to 6
Outputs:
- projected: bfloat16 [65536, 512], P(('blk', 'rep'))
- activated: bfloat16 [65536, 512], P(('blk', 'rep'))
- feature_grad: bfloat16 [65536, 512], P(('blk', 'rep'))
- weight_grad: float32 [512, 512], replicated
- bias_grad: float32 [512], replicated
Inputs may be any that keep to these rules, and one draw needn't show every extreme that they name: For every partition p and destination e the counts move_plan[p, s, e] over sources s sum to 512; the counts of one source over destinations sum to at most 1024, and some source of every partition sends 64 rows to every destination. `tile_rows`: the 6 row tiles listed for one column tile of a device are distinct.
All inputs are finite; a program needn't handle non-finite values.
Results may differ from a plain program's by a relative error of at most 0.018.
Values may be sent and summed in bfloat16 or wider, within the bound.
No kernel may reach another device: no remote copies, remote signals or barrier semaphores. Data moves between devices by JAX's collectives and lax.ppermute only.
A program may use at most 192 MiB of HBM per device.

v0:
```python
import math
import jax
import jax.numpy as jnp
from jax import lax
from jax.sharding import PartitionSpec as P


def silu_slope(values):
    sigma = jax.nn.sigmoid(values)
    return sigma * (1.0 + values * (1.0 - sigma))


def per_device(raw_features, move_plan, weight, bias_vector, tile_rows, tile_values, grad_out):
    rep_size = lax.axis_size("rep")
    own_index = lax.axis_index("rep")
    dev_rows, feature_width = grad_out.shape
    raw_rows = raw_features.shape[0]
    capacity = 4 * (dev_rows // (2 * rep_size))
    counts = move_plan[0]
    tile_stack = tile_values[0, 0]
    row_lists = tile_rows[0, 0]
    tile_size = tile_stack.shape[2]
    row_tiles = rep_size * dev_rows // tile_size
    root_count = math.sqrt(dev_rows * lax.axis_size("blk") * rep_size)
    sent_counts = lax.dynamic_index_in_dim(counts, own_index, 0, keepdims=False)
    first_rows = jnp.cumsum(sent_counts) - sent_counts
    slot_rows = first_rows[:, None] + jnp.arange(capacity, dtype=jnp.int32)[None, :]
    outgoing = raw_features[jnp.minimum(slot_rows, raw_rows - 1)]
    incoming = lax.all_to_all(outgoing, "rep", split_axis=0, concat_axis=0, tiled=True)
    recv_counts = lax.dynamic_index_in_dim(counts, own_index, 1, keepdims=False)
    inclusive = jnp.cumsum(recv_counts)
    exclusive = inclusive - recv_counts
    positions = jnp.arange(dev_rows, dtype=jnp.int32)
    sources = jnp.sum((inclusive[None, :] <= positions[:, None]).astype(jnp.int32), axis=1)
    selector = sources[:, None] == jnp.arange(rep_size, dtype=jnp.int32)[None, :]
    offsets = jnp.sum(jnp.where(selector, exclusive[None, :], 0), axis=1)
    features = incoming.reshape(rep_size * capacity, feature_width)[
        sources * capacity + positions - offsets
    ]
    projected = jnp.dot(features, weight, preferred_element_type=jnp.float32).astype(jnp.bfloat16)
    zero_rows = jnp.zeros((row_tiles, tile_size, feature_width), jnp.float32)
    shard_rows = lax.all_gather(projected, "blk", axis=0, tiled=True)

    def column_step(step_index, running):
        adjacency_tile = lax.dynamic_index_in_dim(tile_stack, step_index, 0, keepdims=False)
        targets = lax.dynamic_index_in_dim(row_lists, step_index, 0, keepdims=False)
        inputs = lax.dynamic_slice_in_dim(shard_rows, step_index * tile_size, tile_size, 0)
        matmul_result = jnp.einsum(
            "jab,bf->jaf", adjacency_tile, inputs, preferred_element_type=jnp.float32
        )
        return running.at[targets].add(matmul_result)

    partial_value = lax.fori_loop(0, shard_rows.shape[0] // tile_size, column_step, zero_rows)
    partial_value = partial_value.reshape(row_tiles * tile_size, feature_width)
    preact = (
        lax.psum_scatter(
            partial_value.astype(jnp.bfloat16), "rep", scatter_dimension=0, tiled=True
        ).astype(jnp.float32)
        + bias_vector
    )
    own_grad = (grad_out.astype(jnp.float32) * silu_slope(preact)).astype(jnp.bfloat16)
    pre_grad = lax.all_gather(own_grad, "rep", axis=0, tiled=True)
    activated = jax.nn.silu(preact).astype(jnp.bfloat16)
    grad_tiles = pre_grad.reshape(row_tiles, tile_size, feature_width)
    column_indices = lax.axis_size("blk") * dev_rows // tile_size
    adjacency_tile = tile_stack
    targets = row_lists
    selected_rows = grad_tiles[targets]
    column_contribution = jnp.einsum(
        "nzqm,nzqg->nmg", adjacency_tile, selected_rows, preferred_element_type=jnp.float32
    )
    proj_grad = lax.psum_scatter(
        column_contribution.reshape(column_indices * tile_size, feature_width).astype(jnp.bfloat16),
        "blk",
        scatter_dimension=0,
        tiled=True,
    )
    local_weight = jnp.einsum("nf,ng->fg", features, proj_grad, preferred_element_type=jnp.float32)
    local_bias = jnp.sum(own_grad.astype(jnp.float32), axis=0)
    weight_sum, bias_sum = lax.psum((local_weight, local_bias), ("blk", "rep"))
    feature_grad = jnp.einsum(
        "ng,fg->nf", proj_grad, weight, preferred_element_type=jnp.float32
    ).astype(jnp.bfloat16)
    return (projected, activated, feature_grad, weight_sum / root_count, bias_sum / root_count)


def solution(mesh):
    return jax.shard_map(
        per_device,
        mesh=mesh,
        in_specs=(
            P(("blk", "rep"), None),
            P("blk", None, None),
            P(),
            P(),
            P("blk", "rep", None, None),
            P("blk", "rep", None, None, None, None),
            P(("blk", "rep"), None),
        ),
        out_specs=(
            P(("blk", "rep"), None),
            P(("blk", "rep"), None),
            P(("blk", "rep"), None),
            P(),
            P(),
        ),
        check_vma=False,
    )
```

profile of v0, /device:TPU:1, one launch (start us, length us, event | category | flops | bytes accessed | tf_op | source)
XLA Modules:
  0.0 759.6 jit_solution(11965677881912372824)
XLA Ops:
  14.2 8.4 %all-to-all-start = ((bf16[16,64,512]{2,1,0:T(8,128)(2,1)}), bf16[16,64,512]{2,1,0:T(8,128)(2,1)S(1)}, u32[]{:S(2)}, u32[]{:S(2)}) async-start(bf16[16,64,512]{2,1,0:T(8,128)(2,1)} %bitcast.6), calls=%async_computation | async-start | bytes 2097152 | tf_op jit(solution)/shard_map/all_to_all | solution.py:29
  23.9 15.8 %all-to-all-done = bf16[16,64,512]{2,1,0:T(8,128)(2,1)S(1)} async-done(((bf16[16,64,512]{2,1,0:T(8,128)(2,1)}), bf16[16,64,512]{2,1,0:T(8,128)(2,1)S(1)}, u32[]{:S(2)}, u32[]{:S(2)}) %all-to-all-start) | async-done | bytes 1048608 | tf_op jit(solution)/shard_map/all_to_all | solution.py:29
  43.1 89.0 %all-gather.3.cloned.1.call-done = bf16[4096,512]{1,0:T(8,128)(2,1)} async-done(((bf16[512,512]{1,0:T(8,128)(2,1)}), bf16[4096,512]{1,0:T(8,128)(2,1)}) %all-gather.3.cloned.1.call-update) | async-done | bytes 4194320 | tf_op jit(solution)/shard_map/all_gather | solution.py:42
  132.1 7.9 %broadcast_in_dim.18 = f32[32,256,512]{2,1,0:T(8,128)} broadcast(f32[]{:T(128)} %constant.89.clone.1), dimensions={} | broadcast | bytes 16777220 | tf_op jit(solution)/shard_map/broadcast_in_dim | solution.py:41
  139.9 150.8 %while.13 = (s32[]{:T(128)}, f32[32,256,512]{2,1,0:T(8,128)}, s32[16,6]{1,0:T(8,128)S(1)}, bf16[16,6,256,256]{3,2,1,0:T(8,128)(2,1)}, bf16[4096,512]{1,0:T(8,128...) while((s32[]{:T(128)}, f32[32,256,512]{2,1,0:T(8,128)}, s32[16,6]{1,0:T(8,128)S(1)}, ...), condition=%wide.region_6.7_spmd, body=%wide.region_4.6_spmd.sunk | while | flops 403439648 | bytes 13632219 | solution.py:53
  151.1 7.7 %scatter_fusion = f32[32,256,512]{2,1,0:T(8,128)} fusion(f32[32,256,512]{2,1,0:T(8,128)} %get-tuple-element.171, s32[6]{0:T(128)S(1)} %fusion.24, f32[6,256,512]{2,1,0:T(8,128)S(1)} %fusion.25), kind=kCustom, calls=%fused_computation.3.clone.1 | custom fusion | flops 786432 | bytes 9437208 | tf_op jit(solution)/shard_map/while/body/eval_jaxpr/scatter-add | solution.py:51
  160.6 7.6 %scatter_fusion = f32[32,256,512]{2,1,0:T(8,128)} fusion(f32[32,256,512]{2,1,0:T(8,128)} %get-tuple-element.171, s32[6]{0:T(128)S(1)} %fusion.24, f32[6,256,512]{2,1,0:T(8,128)S(1)} %fusion.25), kind=kCustom, calls=%fused_computation.3.clone.1 | custom fusion | flops 786432 | bytes 9437208 | tf_op jit(solution)/shard_map/while/body/eval_jaxpr/scatter-add | solution.py:51
  170.0 7.7 %scatter_fusion = f32[32,256,512]{2,1,0:T(8,128)} fusion(f32[32,256,512]{2,1,0:T(8,128)} %get-tuple-element.171, s32[6]{0:T(128)S(1)} %fusion.24, f32[6,256,512]{2,1,0:T(8,128)S(1)} %fusion.25), kind=kCustom, calls=%fused_computation.3.clone.1 | custom fusion | flops 786432 | bytes 9437208 | tf_op jit(solution)/shard_map/while/body/eval_jaxpr/scatter-add | solution.py:51
  179.5 7.7 %scatter_fusion = f32[32,256,512]{2,1,0:T(8,128)} fusion(f32[32,256,512]{2,1,0:T(8,128)} %get-tuple-element.171, s32[6]{0:T(128)S(1)} %fusion.24, f32[6,256,512]{2,1,0:T(8,128)S(1)} %fusion.25), kind=kCustom, calls=%fused_computation.3.clone.1 | custom fusion | flops 786432 | bytes 9437208 | tf_op jit(solution)/shard_map/while/body/eval_jaxpr/scatter-add | solution.py:51
  198.3 7.7 %scatter_fusion = f32[32,256,512]{2,1,0:T(8,128)} fusion(f32[32,256,512]{2,1,0:T(8,128)} %get-tuple-element.171, s32[6]{0:T(128)S(1)} %fusion.24, f32[6,256,512]{2,1,0:T(8,128)S(1)} %fusion.25), kind=kCustom, calls=%fused_computation.3.clone.1 | custom fusion | flops 786432 | bytes 9437208 | tf_op jit(solution)/shard_map/while/body/eval_jaxpr/scatter-add | solution.py:51
  226.5 7.6 %scatter_fusion = f32[32,256,512]{2,1,0:T(8,128)} fusion(f32[32,256,512]{2,1,0:T(8,128)} %get-tuple-element.171, s32[6]{0:T(128)S(1)} %fusion.24, f32[6,256,512]{2,1,0:T(8,128)S(1)} %fusion.25), kind=kCustom, calls=%fused_computation.3.clone.1 | custom fusion | flops 786432 | bytes 9437208 | tf_op jit(solution)/shard_map/while/body/eval_jaxpr/scatter-add | solution.py:51
  235.9 7.7 %scatter_fusion = f32[32,256,512]{2,1,0:T(8,128)} fusion(f32[32,256,512]{2,1,0:T(8,128)} %get-tuple-element.171, s32[6]{0:T(128)S(1)} %fusion.24, f32[6,256,512]{2,1,0:T(8,128)S(1)} %fusion.25), kind=kCustom, calls=%fused_computation.3.clone.1 | custom fusion | flops 786432 | bytes 9437208 | tf_op jit(solution)/shard_map/while/body/eval_jaxpr/scatter-add | solution.py:51
  245.4 7.6 %scatter_fusion = f32[32,256,512]{2,1,0:T(8,128)} fusion(f32[32,256,512]{2,1,0:T(8,128)} %get-tuple-element.171, s32[6]{0:T(128)S(1)} %fusion.24, f32[6,256,512]{2,1,0:T(8,128)S(1)} %fusion.25), kind=kCustom, calls=%fused_computation.3.clone.1 | custom fusion | flops 786432 | bytes 9437208 | tf_op jit(solution)/shard_map/while/body/eval_jaxpr/scatter-add | solution.py:51
  254.8 7.7 %scatter_fusion = f32[32,256,512]{2,1,0:T(8,128)} fusion(f32[32,256,512]{2,1,0:T(8,128)} %get-tuple-element.171, s32[6]{0:T(128)S(1)} %fusion.24, f32[6,256,512]{2,1,0:T(8,128)S(1)} %fusion.25), kind=kCustom, calls=%fused_computation.3.clone.1 | custom fusion | flops 786432 | bytes 9437208 | tf_op jit(solution)/shard_map/while/body/eval_jaxpr/scatter-add | solution.py:51
  264.3 7.6 %scatter_fusion = f32[32,256,512]{2,1,0:T(8,128)} fusion(f32[32,256,512]{2,1,0:T(8,128)} %get-tuple-element.171, s32[6]{0:T(128)S(1)} %fusion.24, f32[6,256,512]{2,1,0:T(8,128)S(1)} %fusion.25), kind=kCustom, calls=%fused_computation.3.clone.1 | custom fusion | flops 786432 | bytes 9437208 | tf_op jit(solution)/shard_map/while/body/eval_jaxpr/scatter-add | solution.py:51
  283.1 7.6 %scatter_fusion = f32[32,256,512]{2,1,0:T(8,128)} fusion(f32[32,256,512]{2,1,0:T(8,128)} %get-tuple-element.171, s32[6]{0:T(128)S(1)} %fusion.24, f32[6,256,512]{2,1,0:T(8,128)S(1)} %fusion.25), kind=kCustom, calls=%fused_computation.3.clone.1 | custom fusion | flops 786432 | bytes 9437208 | tf_op jit(solution)/shard_map/while/body/eval_jaxpr/scatter-add | solution.py:51
  290.7 9.1 %convert_element_type.41 = bf16[32,256,512]{2,1,0:T(8,128)(2,1)} convert(f32[32,256,512]{2,1,0:T(8,128)} %get-tuple-element.99) | non-fusion elementwise | flops 4194304 | bytes 25165824 | tf_op jit(solution)/shard_map/convert_element_type | solution.py:57
  299.9 101.1 %reduce-scatter.3.cloned.1.call-done = bf16[512,512]{1,0:T(8,128)(2,1)} async-done(((bf16[8192,512]{1,0:T(8,128)(2,1)}), bf16[512,512]{1,0:T(8,128)(2,1)}) %reduce-scatter.3.cloned.1.call-update) | async-done | bytes 524304 | tf_op jit(solution)/shard_map/reduce_scatter | solution.py:56
  403.8 73.5 %all-gather.5.cloned.1.call-done = bf16[8192,512]{1,0:T(8,128)(2,1)} async-done(((bf16[512,512]{1,0:T(8,128)(2,1)}), bf16[8192,512]{1,0:T(8,128)(2,1)}) %all-gather.5.cloned.1.call-update) | async-done | bytes 8388624 | tf_op jit(solution)/shard_map/all_gather | solution.py:62
  477.3 13.6 %gather_fusion.2 = bf16[96,256,512]{2,1,0:T(8,128)(2,1)} fusion(bf16[32,256,512]{2,1,0:T(8,128)(2,1)} %bitcast.59, s32[1024]{0:T(1024)S(1)} %pad_clamp_fusion), kind=kCustom, calls=%fused_computation.2 | custom fusion | bytes 50332032 | tf_op jit(solution)/shard_map/gather | solution.py:68
  490.9 17.4 %bitcast_convert_fusion = bf16[16,512,256]{1,2,0:T(8,128)(2,1)} fusion(bf16[16,6,256,512]{3,2,1,0:T(8,128)(2,1)} %bitcast.62, bf16[1,1,16,6,256,256]{5,4,3,2,1,0:T(8,128)(2,1)} %bitcast.65), kind=kOutput, calls=%fused_computation.14 | convolution fusion | flops 6444548096 | bytes 41943040 | tf_op jit(solution)/shard_map/nzqm,nzqg->nmg/dot_general | solution.py:69
  508.4 88.7 %reduce-scatter.5.cloned.1.call-done = bf16[512,512]{1,0:T(8,128)(2,1)} async-done(((bf16[4096,512]{1,0:T(8,128)(2,1)}), bf16[512,512]{1,0:T(8,128)(2,1)}) %reduce-scatter.5.cloned.1.call-update) | async-done | bytes 524304 | tf_op jit(solution)/shard_map/reduce_scatter | solution.py:72
  599.6 64.9 %psum.15 = f32[512]{0:T(512)S(1)} all-reduce(f32[512]{0:T(512)S(1)} %get-tuple-element.125), channel_id=1, replica_groups=mesh['blk'=8,'rep'=16] {'blk','rep'}, use_global_device_ids=true, to_apply=%region_11.12 | all-reduce | flops 512 | bytes 4096 | tf_op jit(solution)/shard_map/psum | solution.py:80
  667.4 83.4 %all-reduce.2.cloned.1.call-done = f32[512,512]{1,0:T(8,128)} async-done(((f32[512,512]{1,0:T(8,128)}), f32[512,512]{1,0:T(8,128)}) %all-reduce.2.cloned.1.call-update) | async-done | bytes 1048592 | tf_op jit(solution)/shard_map/psum | solution.py:80
  (95 shorter events, 88.4 us)
Async XLA Ops:
  7.2 1.9 copy-start
  7.2 34.5 %copy-start.4 = (bf16[512,512]{1,0:T(8,128)(2,1)S(1)}, bf16[512,512]{1,0:T(8,128)(2,1)}, u32[]{:S(2)}) copy-start(bf16[512,512]{1,0:T(8,128)(2,1)} %param.11) | copy-start | bytes 1572868
  7.2 35.8 %copy-start.7 = (s32[1,1,16,6]{2,1,3,0:T(1,128)S(1)}, s32[1,1,16,6]{2,1,3,0:T(1,128)}, u32[]{:S(2)}) copy-start(s32[1,1,16,6]{2,1,3,0:T(1,128)} %param.13) | copy-start | bytes 1156
  14.2 25.5 %all-to-all-start = ((bf16[16,64,512]{2,1,0:T(8,128)(2,1)}), bf16[16,64,512]{2,1,0:T(8,128)(2,1)S(1)}, u32[]{:S(2)}, u32[]{:S(2)}) async-start(bf16[16,64,512]{2,1,0:T(8,128)(2,1)} %bitcast.6), calls=%async_computation | async-start | bytes 2097152 | tf_op jit(solution)/shard_map/all_to_all | solution.py:29
  22.6 109.4 %all-gather.3.cloned.1.call-start = ((), (), s32[]{:S(2)}) async-start(), calls=%async_computation.3 | async-start | bytes 4718592 | tf_op jit(solution)/shard_map/all_gather | solution.py:42
  41.7 98.2 %copy-start.2 = (bf16[512,512]{1,0:T(8,128)(2,1)}, bf16[512,512]{1,0:T(8,128)(2,1)S(1)}, u32[]{:S(2)}) copy-start(bf16[512,512]{1,0:T(8,128)(2,1)S(1)} %gather_fusion.1) | copy-start | bytes 1572868
  43.0 358.1 %reduce-scatter.3.cloned.1.call-start = ((), (), s32[]{:S(2)}) async-start(), calls=%async_computation.4 | async-start | bytes 8912896 | tf_op jit(solution)/shard_map/reduce_scatter | solution.py:56
  290.7 110.3 %copy-start.6 = (bf16[512,512]{1,0:T(8,128)(2,1)S(1)}, bf16[512,512]{1,0:T(8,128)(2,1)}, u32[]{:S(2)}) copy-start(bf16[512,512]{1,0:T(8,128)(2,1)} %param.15) | copy-start | bytes 1572868
  290.7 110.3 %copy-start.8 = (f32[512]{0:T(512)S(1)}, f32[512]{0:T(512)}, u32[]{:S(2)}) copy-start(f32[512]{0:T(512)} %param.12) | copy-start | bytes 6148
  299.9 177.4 %all-gather.5.cloned.1.call-start = ((), (), s32[]{:S(2)}) async-start(), calls=%async_computation.5 | async-start | bytes 8912896 | tf_op jit(solution)/shard_map/all_gather | solution.py:62
  403.6 193.5 %reduce-scatter.5.cloned.1.call-start = ((), (), s32[]{:S(2)}) async-start(), calls=%async_computation.6 | async-start | bytes 4718592 | tf_op jit(solution)/shard_map/reduce_scatter | solution.py:72
  490.9 106.2 %copy-start.3 = (bf16[512,512]{1,0:T(8,128)(2,1)S(1)}, bf16[512,512]{1,0:T(8,128)(2,1)}, u32[]{:S(2)}) copy-start(bf16[512,512]{1,0:T(8,128)(2,1)} %copy-done.2) | copy-start | bytes 1572868
  490.9 174.1 %copy-start.5 = (bf16[512,512]{1,0:T(8,128)(2,1)S(1)}, bf16[512,512]{1,0:T(8,128)(2,1)}, u32[]{:S(2)}) copy-start(bf16[512,512]{1,0:T(8,128)(2,1)} %param.11) | copy-start | bytes 1572868
  490.9 262.1 %copy-start.1 = (bf16[1024,512]{1,0:T(8,128)(2,1)S(1)}, bf16[1024,512]{1,0:T(8,128)(2,1)}, u32[]{:S(2)}) copy-start(bf16[1024,512]{1,0:T(8,128)(2,1)} %param.9) | copy-start | bytes 3145732
  508.3 242.5 %all-reduce.2.cloned.1.call-start = ((), (), s32[]{:S(2)}) async-start(), calls=%async_computation.7 | async-start | bytes 2097152 | tf_op jit(solution)/shard_map/psum | solution.py:80
Sparse Core Ops, SparseCore 0:
  43.1 88.9 all-gather.2
  300.0 100.9 reduce-scatter.2
  404.1 73.2 all-gather.4
  508.4 88.5 reduce-scatter.4
  602.3 148.4 all-reduce.1
where the time goes:
time: 762 us; the launch traced here: 760 us
  waiting for transfers between devices  452 us (59%)
  other arithmetic  138 us (18%)
  blocking collectives  64.9 us (9%)
  matrix products  51.4 us (7%)
  local copies, waits for them, and re-layouts  30.6 us (4%)
  between operations  13.9 us (2%)
  starting transfers between devices  8.64 us (1%)
    scatter-add x16, other arithmetic, column_step(): return running.at[targets].add(matmul_result)  122 us
    reduce_scatter x1, waiting for transfers between devices, per_device(): lax.psum_scatter(partial_value.astype(jnp.bfloat16), 'rep', scatter_dimen...  101 us
    all_gather x1, waiting for transfers between devices, per_device(): shard_rows = lax.all_gather(projected, 'blk', axis=0, tiled=True)  89 us
    reduce_scatter x1, waiting for transfers between devices, per_device(): lax.psum_scatter(column_contribution.reshape(column_indices * tile_size,...  88.7 us
    psum x1, waiting for transfers between devices, per_device(): weight_sum, bias_sum = lax.psum((local_weight, local_bias), ('blk', 'rep'))  83.4 us
    all_gather x1, waiting for transfers between devices, per_device(): pre_grad = lax.all_gather(own_grad, 'rep', axis=0, tiled=True)  73.5 us
    psum x1, blocking collectives, per_device(): weight_sum, bias_sum = lax.psum((local_weight, local_bias), ('blk', 'rep'))  64.9 us
    dot_general x16, matrix products, column_step(): jnp.einsum('jab,bf->jaf', adjacency_tile, inputs, preferred_element_type=...  28 us
  transfers between devices with their start and end apart: 6, of which 6 were waited for; matrix products, arithmetic and copies ran while one was open for 1% of the time, Pallas kernels for 0%

commit v1 on v0

--- a/solution.py
+++ b/solution.py
@@ -39,7 +39,15 @@
     ]
     projected = jnp.dot(features, weight, preferred_element_type=jnp.float32).astype(jnp.bfloat16)
     zero_rows = jnp.zeros((row_tiles, tile_size, feature_width), jnp.float32)
-    shard_rows = lax.all_gather(projected, "blk", axis=0, tiled=True)
+    shard_rows = jnp.concatenate(
+        lax.all_to_all(
+            jnp.stack([projected for _ in range(lax.psum(1, "blk"))], axis=0),
+            "blk",
+            split_axis=0,
+            concat_axis=0,
+        ),
+        axis=0,
+    )
 
     def column_step(step_index, running):
         adjacency_tile = lax.dynamic_index_in_dim(tile_stack, step_index, 0, keepdims=False)

time: 762 us -> 727 us (0.954)
  waiting for transfers between devices: 452 us -> 409 us
    all_gather x1 -> x0, waiting for transfers between devices: 89 us -> none  [per_device(): shard_rows = lax.all_gather(projected, 'blk', axis=0, tiled=True)]
    all_to_all x0 -> x1, waiting for transfers between devices: none -> 48.2 us  [per_device(): lax.all_to_all(jnp.stack([projected for _ in range(lax.psum(1, 'blk'))],...]
where the time goes in v1:
time: 727 us; the launch traced here: 725 us
  waiting for transfers between devices  409 us (56%)
  other arithmetic  138 us (19%)
  blocking collectives  64.9 us (9%)
  matrix products  50.6 us (7%)
  local copies, waits for them, and re-layouts  33.7 us (5%)
  between operations  13.9 us (2%)
  starting transfers between devices  13.8 us (2%)
    scatter-add x16, other arithmetic, column_step(): return running.at[targets].add(matmul_result)  122 us
    reduce_scatter x1, waiting for transfers between devices, per_device(): lax.psum_scatter(partial_value.astype(jnp.bfloat16), 'rep', scatter_dimen...  99.3 us
    reduce_scatter x1, waiting for transfers between devices, per_device(): lax.psum_scatter(column_contribution.reshape(column_indices * tile_size,...  88.7 us
    psum x1, waiting for transfers between devices, per_device(): weight_sum, bias_sum = lax.psum((local_weight, local_bias), ('blk', 'rep'))  83.5 us
    all_gather x1, waiting for transfers between devices, per_device(): pre_grad = lax.all_gather(own_grad, 'rep', axis=0, tiled=True)  73.5 us
    psum x1, blocking collectives, per_device(): weight_sum, bias_sum = lax.psum((local_weight, local_bias), ('blk', 'rep'))  64.9 us
    all_to_all x1, waiting for transfers between devices, per_device(): lax.all_to_all(jnp.stack([projected for _ in range(lax.psum(1, 'blk'))],...  48.2 us
    dot_general x16, matrix products, column_step(): jnp.einsum('jab,bf->jaf', adjacency_tile, inputs, preferred_element_type=...  28 us
  transfers between devices with their start and end apart: 6, of which 6 were waited for; matrix products, arithmetic and copies ran while one was open for 1% of the time, Pallas kernels for 0%

profile of v1, /device:TPU:1, one launch (start us, length us, event | category | flops | bytes accessed | tf_op | source)
XLA Modules:
  0.0 724.7 jit_solution(4416835266004581956)
XLA Ops:
  14.2 8.6 %all-to-all-start = ((bf16[16,64,512]{2,1,0:T(8,128)(2,1)}), bf16[16,64,512]{2,1,0:T(8,128)(2,1)S(1)}, u32[]{:S(2)}, u32[]{:S(2)}) async-start(bf16[16,64,512]{2,1,0:T(8,128)(2,1)} %bitcast.6), calls=%async_computation | async-start | bytes 2097152 | tf_op jit(solution)/shard_map/all_to_all | solution.py:29
  24.0 15.8 %all-to-all-done = bf16[16,64,512]{2,1,0:T(8,128)(2,1)S(1)} async-done(((bf16[16,64,512]{2,1,0:T(8,128)(2,1)}), bf16[16,64,512]{2,1,0:T(8,128)(2,1)S(1)}, u32[]{:S(2)}, u32[]{:S(2)}) %all-to-all-start) | async-done | bytes 1048608 | tf_op jit(solution)/shard_map/all_to_all | solution.py:29
  50.6 48.2 %all-to-all-done.1 = bf16[8,512,512]{2,1,0:T(8,128)(2,1)} async-done(((bf16[8,512,512]{2,1,0:T(8,128)(2,1)}), bf16[8,512,512]{2,1,0:T(8,128)(2,1)}, u32[]{:S(2)}, u32[]{:S(2)}) %all-to-all-start.1) | async-done | bytes 4194336 | tf_op jit(solution)/shard_map/all_to_all | solution.py:43
  98.8 7.9 %broadcast_in_dim.18 = f32[32,256,512]{2,1,0:T(8,128)} broadcast(f32[]{:T(128)} %constant.89.clone.1), dimensions={} | broadcast | bytes 16777220 | tf_op jit(solution)/shard_map/broadcast_in_dim | solution.py:41
  106.7 150.8 %while.13 = (s32[]{:T(128)}, f32[32,256,512]{2,1,0:T(8,128)}, s32[16,6]{1,0:T(8,128)S(1)}, bf16[16,6,256,256]{3,2,1,0:T(8,128)(2,1)}, bf16[4096,512]{1,0:T(8,128...) while((s32[]{:T(128)}, f32[32,256,512]{2,1,0:T(8,128)}, s32[16,6]{1,0:T(8,128)S(1)}, ...), condition=%wide.region_6.7_spmd, body=%wide.region_4.6_spmd.sunk | while | flops 403439648 | bytes 13632219 | solution.py:61
  117.8 7.7 %scatter_fusion = f32[32,256,512]{2,1,0:T(8,128)} fusion(f32[32,256,512]{2,1,0:T(8,128)} %get-tuple-element.171, s32[6]{0:T(128)S(1)} %fusion.24, f32[6,256,512]{2,1,0:T(8,128)S(1)} %fusion.25), kind=kCustom, calls=%fused_computation.3.clone.1 | custom fusion | flops 786432 | bytes 9437208 | tf_op jit(solution)/shard_map/while/body/eval_jaxpr/scatter-add | solution.py:59
  127.3 7.6 %scatter_fusion = f32[32,256,512]{2,1,0:T(8,128)} fusion(f32[32,256,512]{2,1,0:T(8,128)} %get-tuple-element.171, s32[6]{0:T(128)S(1)} %fusion.24, f32[6,256,512]{2,1,0:T(8,128)S(1)} %fusion.25), kind=kCustom, calls=%fused_computation.3.clone.1 | custom fusion | flops 786432 | bytes 9437208 | tf_op jit(solution)/shard_map/while/body/eval_jaxpr/scatter-add | solution.py:59
  136.7 7.7 %scatter_fusion = f32[32,256,512]{2,1,0:T(8,128)} fusion(f32[32,256,512]{2,1,0:T(8,128)} %get-tuple-element.171, s32[6]{0:T(128)S(1)} %fusion.24, f32[6,256,512]{2,1,0:T(8,128)S(1)} %fusion.25), kind=kCustom, calls=%fused_computation.3.clone.1 | custom fusion | flops 786432 | bytes 9437208 | tf_op jit(solution)/shard_map/while/body/eval_jaxpr/scatter-add | solution.py:59
  146.2 7.7 %scatter_fusion = f32[32,256,512]{2,1,0:T(8,128)} fusion(f32[32,256,512]{2,1,0:T(8,128)} %get-tuple-element.171, s32[6]{0:T(128)S(1)} %fusion.24, f32[6,256,512]{2,1,0:T(8,128)S(1)} %fusion.25), kind=kCustom, calls=%fused_computation.3.clone.1 | custom fusion | flops 786432 | bytes 9437208 | tf_op jit(solution)/shard_map/while/body/eval_jaxpr/scatter-add | solution.py:59
  165.0 7.7 %scatter_fusion = f32[32,256,512]{2,1,0:T(8,128)} fusion(f32[32,256,512]{2,1,0:T(8,128)} %get-tuple-element.171, s32[6]{0:T(128)S(1)} %fusion.24, f32[6,256,512]{2,1,0:T(8,128)S(1)} %fusion.25), kind=kCustom, calls=%fused_computation.3.clone.1 | custom fusion | flops 786432 | bytes 9437208 | tf_op jit(solution)/shard_map/while/body/eval_jaxpr/scatter-add | solution.py:59
  193.2 7.6 %scatter_fusion = f32[32,256,512]{2,1,0:T(8,128)} fusion(f32[32,256,512]{2,1,0:T(8,128)} %get-tuple-element.171, s32[6]{0:T(128)S(1)} %fusion.24, f32[6,256,512]{2,1,0:T(8,128)S(1)} %fusion.25), kind=kCustom, calls=%fused_computation.3.clone.1 | custom fusion | flops 786432 | bytes 9437208 | tf_op jit(solution)/shard_map/while/body/eval_jaxpr/scatter-add | solution.py:59
  202.7 7.7 %scatter_fusion = f32[32,256,512]{2,1,0:T(8,128)} fusion(f32[32,256,512]{2,1,0:T(8,128)} %get-tuple-element.171, s32[6]{0:T(128)S(1)} %fusion.24, f32[6,256,512]{2,1,0:T(8,128)S(1)} %fusion.25), kind=kCustom, calls=%fused_computation.3.clone.1 | custom fusion | flops 786432 | bytes 9437208 | tf_op jit(solution)/shard_map/while/body/eval_jaxpr/scatter-add | solution.py:59
  212.1 7.6 %scatter_fusion = f32[32,256,512]{2,1,0:T(8,128)} fusion(f32[32,256,512]{2,1,0:T(8,128)} %get-tuple-element.171, s32[6]{0:T(128)S(1)} %fusion.24, f32[6,256,512]{2,1,0:T(8,128)S(1)} %fusion.25), kind=kCustom, calls=%fused_computation.3.clone.1 | custom fusion | flops 786432 | bytes 9437208 | tf_op jit(solution)/shard_map/while/body/eval_jaxpr/scatter-add | solution.py:59
  221.6 7.7 %scatter_fusion = f32[32,256,512]{2,1,0:T(8,128)} fusion(f32[32,256,512]{2,1,0:T(8,128)} %get-tuple-element.171, s32[6]{0:T(128)S(1)} %fusion.24, f32[6,256,512]{2,1,0:T(8,128)S(1)} %fusion.25), kind=kCustom, calls=%fused_computation.3.clone.1 | custom fusion | flops 786432 | bytes 9437208 | tf_op jit(solution)/shard_map/while/body/eval_jaxpr/scatter-add | solution.py:59
  231.0 7.6 %scatter_fusion = f32[32,256,512]{2,1,0:T(8,128)} fusion(f32[32,256,512]{2,1,0:T(8,128)} %get-tuple-element.171, s32[6]{0:T(128)S(1)} %fusion.24, f32[6,256,512]{2,1,0:T(8,128)S(1)} %fusion.25), kind=kCustom, calls=%fused_computation.3.clone.1 | custom fusion | flops 786432 | bytes 9437208 | tf_op jit(solution)/shard_map/while/body/eval_jaxpr/scatter-add | solution.py:59
  249.8 7.6 %scatter_fusion = f32[32,256,512]{2,1,0:T(8,128)} fusion(f32[32,256,512]{2,1,0:T(8,128)} %get-tuple-element.171, s32[6]{0:T(128)S(1)} %fusion.24, f32[6,256,512]{2,1,0:T(8,128)S(1)} %fusion.25), kind=kCustom, calls=%fused_computation.3.clone.1 | custom fusion | flops 786432 | bytes 9437208 | tf_op jit(solution)/shard_map/while/body/eval_jaxpr/scatter-add | solution.py:59
  257.5 9.1 %convert_element_type.41 = bf16[32,256,512]{2,1,0:T(8,128)(2,1)} convert(f32[32,256,512]{2,1,0:T(8,128)} %get-tuple-element.99) | non-fusion elementwise | flops 4194304 | bytes 25165824 | tf_op jit(solution)/shard_map/convert_element_type | solution.py:65
  266.7 99.3 %reduce-scatter.3.cloned.1.call-done = bf16[512,512]{1,0:T(8,128)(2,1)} async-done(((bf16[8192,512]{1,0:T(8,128)(2,1)}), bf16[512,512]{1,0:T(8,128)(2,1)}) %reduce-scatter.3.cloned.1.call-update) | async-done | bytes 524304 | tf_op jit(solution)/shard_map/reduce_scatter | solution.py:64
  368.8 73.5 %all-gather.2.cloned.1.call-done = bf16[8192,512]{1,0:T(8,128)(2,1)} async-done(((bf16[512,512]{1,0:T(8,128)(2,1)}), bf16[8192,512]{1,0:T(8,128)(2,1)}) %all-gather.2.cloned.1.call-update) | async-done | bytes 8388624 | tf_op jit(solution)/shard_map/all_gather | solution.py:70
  442.3 13.6 %gather_fusion.2 = bf16[96,256,512]{2,1,0:T(8,128)(2,1)} fusion(bf16[32,256,512]{2,1,0:T(8,128)(2,1)} %bitcast.60, s32[1024]{0:T(1024)S(1)} %pad_clamp_fusion), kind=kCustom, calls=%fused_computation.2 | custom fusion | bytes 50332032 | tf_op jit(solution)/shard_map/gather | solution.py:76
  455.9 17.4 %bitcast_convert_fusion = bf16[16,512,256]{1,2,0:T(8,128)(2,1)} fusion(bf16[16,6,256,512]{3,2,1,0:T(8,128)(2,1)} %bitcast.63, bf16[1,1,16,6,256,256]{5,4,3,2,1,0:T(8,128)(2,1)} %bitcast.66), kind=kOutput, calls=%fused_computation.14 | convolution fusion | flops 6444548096 | bytes 41943040 | tf_op jit(solution)/shard_map/nzqm,nzqg->nmg/dot_general | solution.py:77
  473.4 88.7 %reduce-scatter.5.cloned.1.call-done = bf16[512,512]{1,0:T(8,128)(2,1)} async-done(((bf16[4096,512]{1,0:T(8,128)(2,1)}), bf16[512,512]{1,0:T(8,128)(2,1)}) %reduce-scatter.5.cloned.1.call-update) | async-done | bytes 524304 | tf_op jit(solution)/shard_map/reduce_scatter | solution.py:80
  564.6 64.9 %psum.15 = f32[512]{0:T(512)S(1)} all-reduce(f32[512]{0:T(512)S(1)} %get-tuple-element.125), channel_id=1, replica_groups=mesh['blk'=8,'rep'=16] {'blk','rep'}, use_global_device_ids=true, to_apply=%region_11.12 | all-reduce | flops 512 | bytes 4096 | tf_op jit(solution)/shard_map/psum | solution.py:88
  632.3 83.5 %all-reduce.2.cloned.1.call-done = f32[512,512]{1,0:T(8,128)} async-done(((f32[512,512]{1,0:T(8,128)}), f32[512,512]{1,0:T(8,128)}) %all-reduce.2.cloned.1.call-update) | async-done | bytes 1048592 | tf_op jit(solution)/shard_map/psum | solution.py:88
  (97 shorter events, 95.8 us)
Async XLA Ops:
  7.2 1.9 copy-start
  7.2 34.6 %copy-start.4 = (bf16[512,512]{1,0:T(8,128)(2,1)S(1)}, bf16[512,512]{1,0:T(8,128)(2,1)}, u32[]{:S(2)}) copy-start(bf16[512,512]{1,0:T(8,128)(2,1)} %param.11) | copy-start | bytes 1572868
  14.2 36.3 %copy-start.8 = (s32[1,1,16,6]{2,1,3,0:T(1,128)S(1)}, s32[1,1,16,6]{2,1,3,0:T(1,128)}, u32[]{:S(2)}) copy-start(s32[1,1,16,6]{2,1,3,0:T(1,128)} %param.13) | copy-start | bytes 1156
  14.2 25.6 %all-to-all-start = ((bf16[16,64,512]{2,1,0:T(8,128)(2,1)}), bf16[16,64,512]{2,1,0:T(8,128)(2,1)S(1)}, u32[]{:S(2)}, u32[]{:S(2)}) async-start(bf16[16,64,512]{2,1,0:T(8,128)(2,1)} %bitcast.6), calls=%async_computation | async-start | bytes 2097152 | tf_op jit(solution)/shard_map/all_to_all | solution.py:29
  41.8 64.9 %copy-start.2 = (bf16[512,512]{1,0:T(8,128)(2,1)}, bf16[512,512]{1,0:T(8,128)(2,1)S(1)}, u32[]{:S(2)}) copy-start(bf16[512,512]{1,0:T(8,128)(2,1)S(1)} %gather_fusion.1) | copy-start | bytes 1572868
  42.3 0.8 copy-start.6
  45.3 53.4 %all-to-all-start.1 = ((bf16[8,512,512]{2,1,0:T(8,128)(2,1)}), bf16[8,512,512]{2,1,0:T(8,128)(2,1)}, u32[]{:S(2)}, u32[]{:S(2)}) async-start(bf16[8,512,512]{2,1,0:T(8,128)(2,1)} %stack.2), calls=%async_computation.1 | async-start | bytes 8388608 | tf_op jit(solution)/shard_map/all_to_all | solution.py:43
  50.4 315.5 %reduce-scatter.3.cloned.1.call-start = ((), (), s32[]{:S(2)}) async-start(), calls=%async_computation.4 | async-start | bytes 8912896 | tf_op jit(solution)/shard_map/reduce_scatter | solution.py:64
  257.5 108.5 %copy-start.7 = (bf16[512,512]{1,0:T(8,128)(2,1)S(1)}, bf16[512,512]{1,0:T(8,128)(2,1)}, u32[]{:S(2)}) copy-start(bf16[512,512]{1,0:T(8,128)(2,1)} %param.15) | copy-start | bytes 1572868
  257.5 108.5 %copy-start.9 = (f32[512]{0:T(512)S(1)}, f32[512]{0:T(512)}, u32[]{:S(2)}) copy-start(f32[512]{0:T(512)} %param.12) | copy-start | bytes 6148
  266.6 175.7 %all-gather.2.cloned.1.call-start = ((), (), s32[]{:S(2)}) async-start(), calls=%async_computation.5 | async-start | bytes 8912896 | tf_op jit(solution)/shard_map/all_gather | solution.py:70
  368.5 193.5 %reduce-scatter.5.cloned.1.call-start = ((), (), s32[]{:S(2)}) async-start(), calls=%async_computation.6 | async-start | bytes 4718592 | tf_op jit(solution)/shard_map/reduce_scatter | solution.py:80
  455.9 106.2 %copy-start.3 = (bf16[512,512]{1,0:T(8,128)(2,1)S(1)}, bf16[512,512]{1,0:T(8,128)(2,1)}, u32[]{:S(2)}) copy-start(bf16[512,512]{1,0:T(8,128)(2,1)} %copy-done.2) | copy-start | bytes 1572868
  455.9 174.1 %copy-start.5 = (bf16[512,512]{1,0:T(8,128)(2,1)S(1)}, bf16[512,512]{1,0:T(8,128)(2,1)}, u32[]{:S(2)}) copy-start(bf16[512,512]{1,0:T(8,128)(2,1)} %param.11) | copy-start | bytes 1572868
  455.9 262.2 %copy-start.1 = (bf16[1024,512]{1,0:T(8,128)(2,1)S(1)}, bf16[1024,512]{1,0:T(8,128)(2,1)}, u32[]{:S(2)}) copy-start(bf16[1024,512]{1,0:T(8,128)(2,1)} %param.9) | copy-start | bytes 3145732
  473.3 242.5 %all-reduce.2.cloned.1.call-start = ((), (), s32[]{:S(2)}) async-start(), calls=%async_computation.7 | async-start | bytes 2097152 | tf_op jit(solution)/shard_map/psum | solution.py:88
Sparse Core Ops, SparseCore 0:
  266.8 99.1 reduce-scatter.2
  369.0 73.2 all-gather.1
  473.4 88.5 reduce-scatter.4
  567.3 148.4 all-reduce.1
